TPU v7x, 256 devices: a whole 4x4x8 slice. The times are simulated.
256 devices in a mesh: seq: 4 (over y), ch: 64 (over x, z, core).
Axes of the slice: x: 4, y: 4, z: 8, core: 2. Of those that a mesh axis runs over, the one named last changes fastest.
Arguments:
- tokens: bfloat16 [1024, 8192], P('seq', 'ch'), may hold values from -6 to 6
- in_weight: bfloat16 [8192, 3, 8192], P(None, None, 'ch'), may hold values from -0.0625 to 0.0625
- short_taps: float32 [3, 3, 8192], P(None, None, 'ch'), may hold values from -3 to 3
- decay_rates: float32 [16, 512], P(None, 'ch'), may hold values from 0.05 to 200
- residues: float32 [16, 512], P(None, 'ch'), may hold values from -0.18 to 0.18
- out_weight: bfloat16 [8192, 8192], P('ch'), may hold values from -0.1875 to 0.1875
Outputs:
- mixed: bfloat16 [1024, 8192], P('seq', 'ch')
All inputs are finite; a program needn't handle non-finite values.
Results may differ from a plain program's by a relative error of at most 0.007.
Values may be sent and summed in bfloat16 or wider, within the bound.
No kernel may reach another device: no remote copies, remote signals or barrier semaphores. Data moves between devices by JAX's collectives and lax.ppermute only.
A program may use at most 64 MiB of HBM per device.

v0:
```python
import math
import jax
import jax.numpy as jnp
from jax import lax
from jax.sharding import PartitionSpec as P

TAPS = 3


def passed_along(block, axis, distance):
    devices = range(lax.axis_size(axis))
    route = [(i - distance, i) for i in devices if i - distance in devices]
    return lax.ppermute(block, axis, route)


def on_device(tokens, in_weight, short_taps, decay_rates, residues, out_weight):
    rows_here = tokens.shape[0]
    width_here = in_weight.shape[2]
    model_width = in_weight.shape[0]
    filter_count = decay_rates.shape[1]
    mode_count = decay_rates.shape[0]
    group_width = width_here // filter_count
    tokens_all = rows_here * lax.axis_size("seq")
    flat_weight = in_weight.reshape(model_width, 3 * width_here)
    gathered = lax.all_gather(tokens, "ch", axis=1, tiled=True)
    projected = jnp.dot(gathered, flat_weight, preferred_element_type=jnp.float32).astype(
        jnp.bfloat16
    )
    previous = passed_along(projected[rows_here - (TAPS - 1) :], "seq", 1)
    padded = jnp.concatenate([previous, projected], axis=0).astype(jnp.float32)
    flat_taps = short_taps.reshape(TAPS, 3 * width_here)
    filtered = jnp.zeros((rows_here, 3 * width_here), jnp.float32)
    for shift_back in range(TAPS):
        filtered = (
            filtered
            + flat_taps[shift_back]
            * padded[TAPS - 1 - shift_back : TAPS - 1 - shift_back + rows_here]
        )
    query_stream = filtered[:, :width_here]
    gated_in = filtered[:, width_here : 2 * width_here] * filtered[:, 2 * width_here :]
    block_len = math.gcd(rows_here, 128)
    block_count = rows_here // block_len
    scaled_rates = decay_rates / tokens_all
    offsets_in = jnp.arange(block_len, dtype=jnp.float32)
    filter_taps = jnp.sum(
        residues[None] * jnp.exp(-scaled_rates[None] * offsets_in[:, None, None]), axis=1
    )
    distance = jnp.arange(block_len)[:, None] - jnp.arange(block_len)[None, :]
    lookup = jnp.maximum(distance, 0)
    toeplitz = jnp.where((distance >= 0)[None], filter_taps.T[:, lookup], 0.0)
    blocks_in = gated_in.reshape(block_count, block_len, filter_count, group_width)
    local_part = jnp.einsum("gts,bsgi->btgi", toeplitz, blocks_in, precision=lax.Precision.HIGHEST)
    end_weights = jnp.exp(-scaled_rates[:, :, None] * (block_len - 1 - offsets_in)[None, None, :])
    block_ends = jnp.einsum(
        "mgs,bsgi->bmgi", end_weights, blocks_in, precision=lax.Precision.HIGHEST
    )
    inner_decay = jnp.exp(-scaled_rates * block_len)[:, :, None]
    running = jnp.zeros((mode_count, filter_count, group_width), jnp.float32)
    starts_list = []
    for block_number in range(block_count):
        starts_list.append(running)
        running = inner_decay * running + block_ends[block_number]
    local_starts = jnp.stack(starts_list, axis=0)
    end_state = running.reshape(mode_count, width_here)
    block_decay = jnp.repeat(jnp.exp(-scaled_rates * rows_here), group_width, axis=1)
    incoming = jnp.zeros((mode_count, width_here), jnp.float32)
    for hop_number in range(lax.axis_size("seq") - 1):
        incoming = passed_along(end_state + block_decay * incoming, "seq", 1)
    block_offsets = (jnp.arange(block_count, dtype=jnp.float32) * block_len)[:, None, None]
    start_decay = jnp.exp(-scaled_rates[None] * block_offsets)
    block_starts = (
        local_starts
        + start_decay[..., None] * incoming.reshape(mode_count, filter_count, group_width)[None]
    )
    carry_weights = residues[None] * jnp.exp(
        -scaled_rates[None] * (offsets_in + 1.0)[:, None, None]
    )
    carried = jnp.einsum(
        "tmg,bmgi->btgi", carry_weights, block_starts, precision=lax.Precision.HIGHEST
    )
    convolved = (local_part + carried).reshape(rows_here, width_here)
    gated_out = (query_stream * convolved).astype(jnp.bfloat16)
    turned = lax.psum_scatter(
        lax.dot_general(
            out_weight, gated_out, (((0,), (1,)), ((), ())), preferred_element_type=jnp.float32
        ),
        "ch",
        scatter_dimension=0,
        tiled=True,
    )
    mixed = turned.T.astype(jnp.bfloat16)
    return mixed


def solution(mesh):
    in_specs = (
        P("seq", "ch"),
        P(None, None, "ch"),
        P(None, None, "ch"),
        P(None, "ch"),
        P(None, "ch"),
        P("ch", None),
    )
    out_specs = P("seq", "ch")
    return jax.shard_map(
        on_device, mesh=mesh, in_specs=in_specs, out_specs=out_specs, check_vma=False
    )
```

profile of v0, /device:TPU:8, one launch (start us, length us, event | category | flops | bytes accessed | tf_op | source)
XLA Modules:
  0.0 342.4 jit_solution(9144535828070933124)
XLA Ops:
  6.5 0.7 all-gather.2.cloned.1.call-update
  7.3 0.0 copy-start.3
  7.3 0.0 copy-start.2
  7.3 0.0 reduce-scatter.2.cloned.1.call-start
  7.3 8.8 %copy.18 = bf16[8192,3,128]{0,2,1:T(8,128)(2,1)} copy(bf16[8192,3,128]{2,0,1:T(8,128)(2,1)} %param.7) | data formatting | bytes 12582912 | tf_op args[1]
  16.1 0.1 multiply_reduce_fusion
  16.3 0.1 multiply_exponential_fusion
  16.4 72.4 %all-gather.2.cloned.1.call-done = bf16[256,8192]{1,0:T(8,128)(2,1)} async-done(((bf16[256,128]{1,0:T(8,128)(2,1)}), bf16[256,8192]{1,0:T(8,128)(2,1)}) %all-gather.2.cloned.1.call-update) | async-done | bytes 4194320 | tf_op jit(solution)/shard_map/all_gather | solution.py:25
  88.8 6.4 %convolution_convert_fusion = bf16[256,384]{1,0:T(8,128)(2,1)S(1)} fusion(bf16[256,8192]{1,0:T(8,128)(2,1)} %all-gather.2.cloned.1.call-done, bf16[8192,384]{0,1:T(8,128)(2,1)} %bitcast.77), kind=kOutput, calls=%fused_computation.2 | convolution fusion | flops 1610711040 | bytes 10682368 | tf_op jit(solution)/shard_map/dot_general | solution.py:26
  95.2 3.4 collective-permute-start
  98.6 2.1 collective-permute-done
  100.7 0.1 fusion.4
  100.9 0.1 copy.19
  101.0 0.1 reshape.78
  101.1 0.3 convolution_bitcast_fusion.1
  101.4 3.4 collective-permute-start.1
  104.9 2.7 collective-permute-done.1
  107.6 3.4 collective-permute-start.2
  111.0 0.1 copy.20
  111.1 54.8 %gather_fusion = f32[16384,8]{1,0:T(8,128)} fusion(f32[8,128]{0,1:T(8,128)S(1)} %bitcast.75, s32[16384]{0:T(1024)S(1)} %bitcast_clamp_fusion), kind=kCustom, calls=%fused_computation | custom fusion | bytes 1114112 | tf_op jit(solution)/shard_map/gather | solution.py:50
  165.9 5.1 %copy.21 = f32[128,128,8]{1,0,2:T(8,128)S(1)} copy(f32[128,128,8]{2,1,0:T(8,128)} %bitcast.76) | data formatting | bytes 1048576 | tf_op jit(solution)/shard_map/gather | solution.py:50
  171.0 0.0 collective-permute-done.2
  171.1 3.1 collective-permute-start.3
  174.2 0.9 fusion.1
  175.1 2.1 collective-permute-done.3
  177.2 0.3 fusion
  177.6 0.1 copy.24
  177.7 0.1 copy.25
  177.8 4.5 %convolution_bitcast_fusion = f32[8192,256]{0,1:T(8,128)} fusion(bf16[128,8192]{1,0:T(8,128)(2,1)S(1)} %copy-done, f32[256,128]{1,0:T(8,128)S(1)} %copy.25, f32[256,384]{1,0:T(8,128)S(1)} %fusion.4), kind=kOutput, calls=%fused_computation.1 | convolution fusion | flops 536936448 | bytes 10747904 | tf_op jit(solution)/shard_map/dot_general | solution.py:84
  182.2 0.0 reduce-scatter.2.cloned.1.call-update
  182.2 151.8 %reduce-scatter.2.cloned.1.call-done = f32[128,256]{0,1:T(8,128)} async-done(((f32[8192,256]{0,1:T(8,128)}), f32[128,256]{0,1:T(8,128)}) %reduce-scatter.2.cloned.1.call-update) | async-done | bytes 131088 | tf_op jit(solution)/shard_map/reduce_scatter | solution.py:83
  334.1 1.5 convert_bitcast_fusion
  (22 shorter events, 0.2 us)
Async XLA Ops:
  6.5 171.2 %copy-start = (bf16[128,8192]{1,0:T(8,128)(2,1)S(1)}, bf16[128,8192]{1,0:T(8,128)(2,1)}, u32[]{:S(2)}) copy-start(bf16[128,8192]{1,0:T(8,128)(2,1)} %param.11) | copy-start | bytes 6291460
  6.5 82.2 %all-gather.2.cloned.1.call-start = ((), (), s32[]{:S(2)}) async-start(), calls=%async_computation.1 | async-start | bytes 4259840 | tf_op jit(solution)/shard_map/all_gather | solution.py:25
  7.3 8.8 %copy-start.3 = (f32[16,8]{0,1:T(8,128)S(1)}, f32[16,8]{0,1:T(8,128)}, u32[]{:S(2)}) copy-start(f32[16,8]{0,1:T(8,128)} %param.9) | copy-start | bytes 1540
  7.3 8.9 %copy-start.2 = (f32[16,8]{0,1:T(8,128)S(1)}, f32[16,8]{0,1:T(8,128)}, u32[]{:S(2)}) copy-start(f32[16,8]{0,1:T(8,128)} %param.10) | copy-start | bytes 1540
  7.3 9.0 %copy-start.1 = (f32[3,3,128]{2,1,0:T(4,128)S(1)}, f32[3,3,128]{2,1,0:T(4,128)}, u32[]{:S(2)}) copy-start(f32[3,3,128]{2,1,0:T(4,128)} %param.8) | copy-start | bytes 13828
  7.3 326.8 %reduce-scatter.2.cloned.1.call-start = ((), (), s32[]{:S(2)}) async-start(), calls=%async_computation.2 | async-start | bytes 8519680 | tf_op jit(solution)/shard_map/reduce_scatter | solution.py:83
  95.2 5.5 %collective-permute-start = (bf16[2,384]{1,0:T(2,128)(2,1)S(1)}, bf16[2,384]{1,0:T(2,128)(2,1)S(1)}, u32[]{:S(2)}, u32[]{:S(2)}) collective-permute-start(bf16[2,384]{1,0:T(2,128)(2,1)S(1)} %slice.53), channel_id=1, source_target_pairs={{0,64},{64,128},{128,192},{1,65},{65,129},{129,193},{2,66},{66,130... | collective-permute-start | bytes 4616 | tf_op jit(solution)/shard_map/ppermute | solution.py:13
  101.4 6.2 %collective-permute-start.1 = (f32[16,128]{0,1:T(8,128)S(1)}, f32[16,128]{0,1:T(8,128)S(1)}, u32[]{:S(2)}, u32[]{:S(2)}) collective-permute-start(f32[16,128]{0,1:T(8,128)S(1)} %get-tuple-element.5), channel_id=1, source_target_pairs={{0,64},{64,128},{128,192},{1,65},{65,129},{129,193},{2,66},{66,130... | collective-permute-start | bytes 24584 | tf_op jit(solution)/shard_map/ppermute | solution.py:13
  107.6 63.4 %collective-permute-start.2 = (f32[16,128]{0,1:T(8,128)S(1)}, f32[16,128]{0,1:T(8,128)S(1)}, u32[]{:S(2)}, u32[]{:S(2)}) collective-permute-start(f32[16,128]{0,1:T(8,128)S(1)} %fusion.15), channel_id=1, source_target_pairs={{0,64},{64,128},{128,192},{1,65},{65,129},{129,193},{2,66},{66,130... | collective-permute-start | bytes 24584 | tf_op jit(solution)/shard_map/ppermute | solution.py:13
  171.1 6.2 %collective-permute-start.3 = (f32[16,128]{0,1:T(8,128)S(1)}, f32[16,128]{0,1:T(8,128)S(1)}, u32[]{:S(2)}, u32[]{:S(2)}) collective-permute-start(f32[16,128]{0,1:T(8,128)S(1)} %fusion.16), channel_id=1, source_target_pairs={{0,64},{64,128},{128,192},{1,65},{65,129},{129,193},{2,66},{66,130... | collective-permute-start | bytes 24584 | tf_op jit(solution)/shard_map/ppermute | solution.py:13
Sparse Core Ops, SparseCore 0:
  9.9 78.8 all-gather.1
  182.4 151.6 reduce-scatter.1
where the time goes:
time: 343 us; the launch traced here: 342 us
  waiting for transfers between devices  232 us (68%)
  local copies, waits for them, and re-layouts  69.1 us (20%)
  between operations  13.7 us (4%)
  starting transfers between devices  13.3 us (4%)
  matrix products  12.4 us (4%)
    reduce_scatter x1, waiting for transfers between devices, on_device(): lax.psum_scatter(lax.dot_general(out_weight, gated_out, (((0,), (1,)), ((...  152 us
    all_gather x1, waiting for transfers between devices, on_device(): gathered = lax.all_gather(tokens, 'ch', axis=1, tiled=True)  72.4 us
    gather x2, local copies, waits for them, and re-layouts, on_device(): toeplitz = jnp.where((distance >= 0)[None], filter_taps.T[:, lookup], 0.0)  59.9 us
    ppermute x4, starting transfers between devices, passed_along(): return lax.ppermute(block, axis, route)  13.3 us
    unnamed x10, local copies, waits for them, and re-layouts  8.78 us
    ppermute x4, waiting for transfers between devices, passed_along(): return lax.ppermute(block, axis, route)  6.93 us
  transfers between devices with their start and end apart: 6, of which 5 were waited for; matrix products, arithmetic and copies ran while one was open for 20% of the time, Pallas kernels for 0%

commit v1 on v0

--- a/solution.py
+++ b/solution.py
@@ -22,7 +22,9 @@
     group_width = width_here // filter_count
     tokens_all = rows_here * lax.axis_size("seq")
     flat_weight = in_weight.reshape(model_width, 3 * width_here)
-    gathered = lax.all_gather(tokens, "ch", axis=1, tiled=True)
+    gathered = jnp.concatenate(
+        lax.all_to_all(jnp.stack([tokens] * lax.axis_size("ch")), "ch", 0, 0), axis=1
+    )
     projected = jnp.dot(gathered, flat_weight, preferred_element_type=jnp.float32).astype(
         jnp.bfloat16
     )

time: 343 us -> 369 us (1.076)
  starting transfers between devices: 13.3 us -> 25.9 us
  waiting for transfers between devices: 232 us -> 242 us
    all_to_all x0 -> x1, waiting for transfers between devices: none -> 86.5 us  [on_device(): lax.all_to_all(jnp.stack([tokens] * lax.axis_size('ch')), 'ch', 0, 0)]
    all_gather x1 -> x0, waiting for transfers between devices: 72.4 us -> none  [on_device(): gathered = lax.all_gather(tokens, 'ch', axis=1, tiled=True)]
    all_to_all x0 -> x1, starting transfers between devices: none -> 12.2 us  [on_device(): lax.all_to_all(jnp.stack([tokens] * lax.axis_size('ch')), 'ch', 0, 0)]
    unnamed x10 -> x11, local copies, waits for them, and re-layouts: 8.78 us -> 9.86 us
  transfers between devices with their start and end apart: 6 -> 6, of which waited for: 5 -> 5; matrix products, arithmetic and copies ran while one was open for 20% -> 19% of each run, Pallas kernels for 0% -> 0%
where the time goes in v1:
time: 369 us; the launch traced here: 368 us
  waiting for transfers between devices  242 us (66%)
  local copies, waits for them, and re-layouts  72.4 us (20%)
  starting transfers between devices  25.9 us (7%)
  between operations  13.7 us (4%)
  matrix products  12.5 us (3%)
    reduce_scatter x1, waiting for transfers between devices, on_device(): lax.psum_scatter(lax.dot_general(out_weight, gated_out, (((0,), (1,)), ((...  149 us
    all_to_all x1, waiting for transfers between devices, on_device(): lax.all_to_all(jnp.stack([tokens] * lax.axis_size('ch')), 'ch', 0, 0)  86.5 us
    gather x2, local copies, waits for them, and re-layouts, on_device(): toeplitz = jnp.where((distance >= 0)[None], filter_taps.T[:, lookup], 0.0)  59.6 us
    ppermute x4, starting transfers between devices, passed_along(): return lax.ppermute(block, axis, route)  13.6 us
    all_to_all x1, starting transfers between devices, on_device(): lax.all_to_all(jnp.stack([tokens] * lax.axis_size('ch')), 'ch', 0, 0)  12.2 us
    unnamed x11, local copies, waits for them, and re-layouts  9.86 us
  transfers between devices with their start and end apart: 6, of which 5 were waited for; matrix products, arithmetic and copies ran while one was open for 19% of the time, Pallas kernels for 0%

profile of v1, /device:TPU:8, one launch (start us, length us, event | category | flops | bytes accessed | tf_op | source)
XLA Modules:
  0.0 368.5 jit_solution(15761244338320215660)
XLA Ops:
  6.5 1.1 copy.19
  7.6 2.6 stack.4
  10.2 12.2 %all-to-all-start = ((bf16[64,256,128]{1,2,0:T(8,128)(2,1)}), bf16[64,256,128]{1,2,0:T(8,128)(2,1)}, u32[]{:S(2)}, u32[]{:S(2)}) async-start(bf16[64,256,128]{1,2,0:T(8,128)(2,1)} %stack.4), calls=%async_computation | async-start | bytes 8388608 | tf_op jit(solution)/shard_map/all_to_all | solution.py:26
  22.4 0.0 copy-start.3
  22.4 0.0 reduce-scatter.2.cloned.1.call-start
  22.5 8.7 %copy.20 = bf16[8192,3,128]{0,2,1:T(8,128)(2,1)} copy(bf16[8192,3,128]{2,0,1:T(8,128)(2,1)} %param.7) | data formatting | bytes 12582912 | tf_op args[1]
  31.3 0.1 multiply_reduce_fusion
  31.4 0.1 multiply_exponential_fusion
  31.5 86.5 %all-to-all-done = bf16[64,256,128]{1,2,0:T(8,128)(2,1)} async-done(((bf16[64,256,128]{1,2,0:T(8,128)(2,1)}), bf16[64,256,128]{1,2,0:T(8,128)(2,1)}, u32[]{:S(2)}, u32[]{:S(2)}) %all-to-all-start) | async-done | bytes 4194336 | tf_op jit(solution)/shard_map/all_to_all | solution.py:26
  118.0 6.4 %convolution_convert_fusion = bf16[256,384]{1,0:T(8,128)(2,1)S(1)} fusion(bf16[256,8192]{0,1:T(8,128)(2,1)} %bitcast.2, bf16[8192,384]{0,1:T(8,128)(2,1)} %bitcast.80), kind=kOutput, calls=%fused_computation.2 | convolution fusion | flops 1610711040 | bytes 10682368 | tf_op jit(solution)/shard_map/dot_general | solution.py:28
  124.4 3.5 collective-permute-start
  127.9 2.0 collective-permute-done
  130.0 0.1 fusion.4
  130.1 0.1 copy.21
  130.2 0.1 reshape.88
  130.3 0.3 convolution_bitcast_fusion.1
  130.7 3.5 collective-permute-start.1
  134.2 2.6 collective-permute-done.1
  136.8 3.5 collective-permute-start.2
  140.3 0.1 copy.22
  140.4 54.4 %gather_fusion = f32[16384,8]{1,0:T(8,128)} fusion(f32[8,128]{0,1:T(8,128)S(1)} %bitcast.78, s32[16384]{0:T(1024)S(1)} %bitcast_clamp_fusion), kind=kCustom, calls=%fused_computation | custom fusion | bytes 1114112 | tf_op jit(solution)/shard_map/gather | solution.py:52
  194.9 5.1 %copy.23 = f32[128,128,8]{1,0,2:T(8,128)S(1)} copy(f32[128,128,8]{2,1,0:T(8,128)} %bitcast.79) | data formatting | bytes 1048576 | tf_op jit(solution)/shard_map/gather | solution.py:52
  200.0 3.2 collective-permute-start.3
  203.2 0.9 fusion.1
  204.2 2.0 collective-permute-done.3
  206.2 0.3 fusion
  206.5 0.1 copy.26
  206.6 0.1 copy.27
  206.7 4.5 %convolution_bitcast_fusion = f32[8192,256]{0,1:T(8,128)} fusion(bf16[128,8192]{1,0:T(8,128)(2,1)S(1)} %copy-done, f32[256,128]{1,0:T(8,128)S(1)} %copy.27, f32[256,384]{1,0:T(8,128)S(1)} %fusion.4), kind=kOutput, calls=%fused_computation.1 | convolution fusion | flops 536936448 | bytes 10747904 | tf_op jit(solution)/shard_map/dot_general | solution.py:86
  211.2 0.0 reduce-scatter.2.cloned.1.call-update
  211.2 148.9 %reduce-scatter.2.cloned.1.call-done = f32[128,256]{0,1:T(8,128)} async-done(((f32[8192,256]{0,1:T(8,128)}), f32[128,256]{0,1:T(8,128)}) %reduce-scatter.2.cloned.1.call-update) | async-done | bytes 131088 | tf_op jit(solution)/shard_map/reduce_scatter | solution.py:85
  360.1 1.5 convert_bitcast_fusion
  (23 shorter events, 0.2 us)
Async XLA Ops:
  6.5 200.2 %copy-start = (bf16[128,8192]{1,0:T(8,128)(2,1)S(1)}, bf16[128,8192]{1,0:T(8,128)(2,1)}, u32[]{:S(2)}) copy-start(bf16[128,8192]{1,0:T(8,128)(2,1)} %param.11) | copy-start | bytes 6291460
  10.2 107.8 %all-to-all-start = ((bf16[64,256,128]{1,2,0:T(8,128)(2,1)}), bf16[64,256,128]{1,2,0:T(8,128)(2,1)}, u32[]{:S(2)}, u32[]{:S(2)}) async-start(bf16[64,256,128]{1,2,0:T(8,128)(2,1)} %stack.4), calls=%async_computation | async-start | bytes 8388608 | tf_op jit(solution)/shard_map/all_to_all | solution.py:26
  22.4 8.8 %copy-start.3 = (f32[16,8]{0,1:T(8,128)S(1)}, f32[16,8]{0,1:T(8,128)}, u32[]{:S(2)}) copy-start(f32[16,8]{0,1:T(8,128)} %param.9) | copy-start | bytes 1540
  22.4 8.8 %copy-start.2 = (f32[16,8]{0,1:T(8,128)S(1)}, f32[16,8]{0,1:T(8,128)}, u32[]{:S(2)}) copy-start(f32[16,8]{0,1:T(8,128)} %param.10) | copy-start | bytes 1540
  22.4 9.0 %copy-start.1 = (f32[3,3,128]{2,1,0:T(4,128)S(1)}, f32[3,3,128]{2,1,0:T(4,128)}, u32[]{:S(2)}) copy-start(f32[3,3,128]{2,1,0:T(4,128)} %param.8) | copy-start | bytes 13828
  22.4 337.6 %reduce-scatter.2.cloned.1.call-start = ((), (), s32[]{:S(2)}) async-start(), calls=%async_computation.2 | async-start | bytes 8519680 | tf_op jit(solution)/shard_map/reduce_scatter | solution.py:85
  124.4 5.5 %collective-permute-start = (bf16[2,384]{1,0:T(2,128)(2,1)S(1)}, bf16[2,384]{1,0:T(2,128)(2,1)S(1)}, u32[]{:S(2)}, u32[]{:S(2)}) collective-permute-start(bf16[2,384]{1,0:T(2,128)(2,1)S(1)} %slice.53), channel_id=1, source_target_pairs={{0,64},{64,128},{128,192},{1,65},{65,129},{129,193},{2,66},{66,130... | collective-permute-start | bytes 4616 | tf_op jit(solution)/shard_map/ppermute | solution.py:13
  130.7 6.2 %collective-permute-start.1 = (f32[16,128]{0,1:T(8,128)S(1)}, f32[16,128]{0,1:T(8,128)S(1)}, u32[]{:S(2)}, u32[]{:S(2)}) collective-permute-start(f32[16,128]{0,1:T(8,128)S(1)} %get-tuple-element.5), channel_id=1, source_target_pairs={{0,64},{64,128},{128,192},{1,65},{65,129},{129,193},{2,66},{66,130... | collective-permute-start | bytes 24584 | tf_op jit(solution)/shard_map/ppermute | solution.py:13
  136.8 63.2 %collective-permute-start.2 = (f32[16,128]{0,1:T(8,128)S(1)}, f32[16,128]{0,1:T(8,128)S(1)}, u32[]{:S(2)}, u32[]{:S(2)}) collective-permute-start(f32[16,128]{0,1:T(8,128)S(1)} %fusion.15), channel_id=1, source_target_pairs={{0,64},{64,128},{128,192},{1,65},{65,129},{129,193},{2,66},{66,130... | collective-permute-start | bytes 24584 | tf_op jit(solution)/shard_map/ppermute | solution.py:13
  200.0 6.2 %collective-permute-start.3 = (f32[16,128]{0,1:T(8,128)S(1)}, f32[16,128]{0,1:T(8,128)S(1)}, u32[]{:S(2)}, u32[]{:S(2)}) collective-permute-start(f32[16,128]{0,1:T(8,128)S(1)} %fusion.16), channel_id=1, source_target_pairs={{0,64},{64,128},{128,192},{1,65},{65,129},{129,193},{2,66},{66,130... | collective-permute-start | bytes 24584 | tf_op jit(solution)/shard_map/ppermute | solution.py:13
Sparse Core Ops, SparseCore 0:
  211.3 148.6 reduce-scatter.1
